TPU v7x, 512 devices: a whole 4x4x16 slice. The times are simulated.
512 devices in a mesh: req: 32 (over y, x, core), grp: 16 (over z).
Axes of the slice: x: 4, y: 4, z: 16, core: 2. Of those that a mesh axis runs over, the one named last changes fastest.
Arguments:
- normed_token_input: bfloat16 [256, 8192], P(None, 'req'), may hold values from -6 to 6
- key_value_weight: bfloat16 [8192, 2048], P('req', 'grp'), may hold values from -0.0625 to 0.0625
- adapter_down_weight: bfloat16 [8192, 128, 128], P('req', 'grp'), may hold values from -0.0625 to 0.0625
- adapter_up_weight: bfloat16 [128, 64, 2048], P(None, None, 'grp'), may hold values from -0.75 to 0.75
- adapter_index_rows: int32 [256, 1], replicated, may hold values from 0 to 127
- queries: bfloat16 [256, 8192], P('req')
- key_value_pages: bfloat16 [10240, 16, 2, 8, 128], P('req', 'grp')
- lengths: int32 [256], P('req'), may hold values from 0 to 511, as said below
- page_slot_table: int32 [256, 32], P('req'), may hold values from 0 to 255, as said below
- departing_slots: int32 [1024], P('req'), may hold values from 0 to 255, as said below
- departing_target: int32 [1024, 1], P('req'), may hold values from 0 to 31; in each aligned block of 32 rows (0 to 31, 32 to 63, ...) at most 2 rows name the same one
Outputs:
- attention: bfloat16 [256, 8192], P('req')
- migrated_pool: bfloat16 [10240, 16, 2, 8, 128], P('req', 'grp')
Inputs may be any that keep to these rules, and one draw needn't show every extreme that they name: `adapter_index_rows`: each row names one adapter; every adapter is named by some request. `lengths`: some request has an empty cache and some has 511 cached tokens. `page_slot_table`: the rows of the requests of one home together name each of that home's slots 0 .. 255 exactly once. `departing_slots`: the 32 entries of one home are distinct. `departing_target`: the 32 rows of one home name one target at most 2 times; some home names some target exactly 2 times.
All inputs are finite; a program needn't handle non-finite values.
Results may differ from a plain program's by a relative error of at most 0.01345.
Values may be sent and summed in bfloat16 or wider, within the bound.
No kernel may reach another device: no remote copies, remote signals or barrier semaphores. Data moves between devices by JAX's collectives and lax.ppermute only.
A program may use at most 64 MiB of HBM per device.

v0:
```python
import math
import jax
import jax.numpy as jnp
from jax import lax
from jax.sharding import PartitionSpec as P

adapter_scale = 2.0
masked_score = -1e30


def shards(
    normed_token_input,
    key_value_weight,
    adapter_down_weight,
    adapter_up_weight,
    adapter_index_rows,
    queries,
    key_value_pages,
    lengths,
    page_slot_table,
    departing_slots,
    departing_target,
):
    selected_adapter = adapter_index_rows[:, 0]
    homes = lax.axis_size("req")
    groups = lax.axis_size("grp")
    home_index = lax.axis_index("req")
    group_index = lax.axis_index("grp")
    rows = lengths.shape[0]
    request_count = normed_token_input.shape[0]
    column_span = key_value_weight.shape[1]
    local_adapters = adapter_down_weight.shape[1]
    rank_width = adapter_down_weight.shape[2]
    rank_half = adapter_up_weight.shape[1]
    slot_tokens = key_value_pages.shape[1]
    heads = key_value_pages.shape[3]
    head_dim = key_value_pages.shape[4]
    key_width = heads * head_dim
    query_heads = queries.shape[1] // head_dim
    heads_per_target = query_heads // groups
    page_size = slot_tokens * groups
    pages = page_slot_table.shape[1]
    both = jnp.concatenate(
        [key_value_weight, adapter_down_weight.reshape(adapter_down_weight.shape[0], -1)], axis=1
    )
    products = jnp.dot(normed_token_input, both, preferred_element_type=jnp.float32)
    base_part = products[:, :column_span]
    down_all = products[:, column_span:].reshape(request_count, local_adapters, rank_width)
    local_choice = selected_adapter - group_index * local_adapters
    picker = (local_choice[:, None] == jnp.arange(local_adapters, dtype=jnp.int32)[None, :]).astype(
        jnp.float32
    )
    mid_part = jnp.einsum("ia,iaw->iw", picker, down_all)
    partial = jnp.concatenate([base_part, mid_part], axis=1).reshape(homes, rows, -1)
    summed = jnp.sum(lax.all_to_all(partial, "req", 0, 0, tiled=False), axis=0)
    base_resident = summed[:, :column_span]
    mid_owned = summed[:, column_span:].astype(jnp.bfloat16)
    resident_adapters = lax.dynamic_slice_in_dim(selected_adapter, home_index * rows, rows)
    owner = resident_adapters // local_adapters
    mid_spread = lax.all_to_all(
        jnp.broadcast_to(mid_owned[None], (groups,) + mid_owned.shape), "grp", 0, 0, tiled=False
    )
    request_index = jnp.arange(rows, dtype=jnp.int32)
    mid_home = mid_spread[owner, request_index]
    is_value = group_index * column_span >= key_width
    mid_used = jnp.where(is_value, mid_home[:, rank_half:], mid_home[:, :rank_half])
    up_weight_rows = adapter_up_weight[resident_adapters]
    adapter_update = jnp.einsum(
        "ir,irc->ic", mid_used, up_weight_rows, preferred_element_type=jnp.float32
    )
    fresh_columns = (base_resident + adapter_scale * adapter_update).astype(jnp.bfloat16)
    gathered = key_value_pages[page_slot_table][:, :, 0]
    keys = gathered[:, :, 0]
    values = gathered[:, :, 1]
    query = queries.reshape(rows, heads, -1, head_dim)
    scores = jnp.einsum(
        "ihgd,inhd->ihgn", query, keys, preferred_element_type=jnp.float32
    ) / math.sqrt(head_dim)
    positions = jnp.arange(pages, dtype=jnp.int32) * page_size + group_index * slot_tokens
    valid = (positions[None, :] < lengths[:, None])[:, None, None, :]
    scores = jnp.where(valid, scores, masked_score)
    local_top = jnp.max(scores, axis=3)
    weights = jnp.where(valid, jnp.exp(scores - local_top[..., None]), 0.0)
    local_total = jnp.sum(weights, axis=3)
    local_mixed = jnp.einsum("ihgn,inhd->ihgd", weights, values, preferred_element_type=jnp.float32)
    parcel = jnp.concatenate(
        [
            local_mixed.reshape(rows, groups, heads_per_target * head_dim),
            local_top.reshape(rows, groups, heads_per_target),
            local_total.reshape(rows, groups, heads_per_target),
            jnp.broadcast_to(
                fresh_columns.astype(jnp.float32)[:, None, :], (rows, groups, column_span)
            ),
        ],
        axis=2,
    ).transpose(1, 0, 2)
    received = lax.all_to_all(parcel, "grp", 0, 0, tiled=False)
    mixed_width = heads_per_target * head_dim
    shard_mixed = received[:, :, :mixed_width].reshape(groups, rows, heads_per_target, head_dim)
    shard_top = received[:, :, mixed_width : mixed_width + heads_per_target]
    shard_total = received[
        :, :, mixed_width + heads_per_target : mixed_width + 2 * heads_per_target
    ]
    new_all = received[:, :, mixed_width + 2 * heads_per_target :].astype(jnp.bfloat16)
    new_all = new_all.transpose(1, 0, 2).reshape(rows, groups * column_span)
    new_keys = new_all[:, :key_width].reshape(rows, heads, head_dim)
    new_values = new_all[:, key_width:].reshape(rows, heads, head_dim)
    head_of_target = group_index * heads_per_target // (query_heads // heads)
    own_query = lax.dynamic_slice_in_dim(
        queries, group_index * mixed_width, mixed_width, axis=1
    ).reshape(rows, heads_per_target, head_dim)
    own_key = lax.dynamic_index_in_dim(new_keys, head_of_target, 1, False)
    own_value = lax.dynamic_index_in_dim(new_values, head_of_target, 1, False)
    new_score = jnp.einsum(
        "ihd,id->ih", own_query, own_key, preferred_element_type=jnp.float32
    ) / math.sqrt(head_dim)
    top = jnp.maximum(jnp.max(shard_top, axis=0), new_score)
    shard_scale = jnp.exp(shard_top - top[None])
    new_weight = jnp.exp(new_score - top)
    total = jnp.sum(shard_total * shard_scale, axis=0) + new_weight
    mixed = (
        jnp.sum(shard_mixed * shard_scale[..., None], axis=0)
        + new_weight[..., None] * own_value.astype(jnp.float32)[:, None, :]
    )
    own_attention = (mixed / total[..., None]).astype(jnp.bfloat16).reshape(rows, mixed_width)
    attention = lax.all_gather(own_attention, "grp", axis=1, tiled=True)
    page_slot = page_slot_table[request_index, lengths // page_size]
    offset = lengths % page_size
    mine = offset // slot_tokens == group_index
    token_local = offset % slot_tokens
    current = key_value_pages[page_slot, token_local]
    fresh = jnp.stack([new_keys, new_values], axis=1)
    written = key_value_pages.at[page_slot, token_local].set(
        jnp.where(mine[:, None, None, None], fresh, current)
    )
    targets = departing_target[:, 0]
    count_out = departing_slots.shape[0]
    order = jnp.arange(count_out, dtype=jnp.int32)
    earlier = (targets[:, None] == targets[None, :]) & (order[None, :] < order[:, None])
    place = jnp.sum(earlier.astype(jnp.int32), axis=1)
    live_slots = rows * pages
    capacity = (key_value_pages.shape[0] - live_slots) // homes
    outbound = (
        jnp.zeros((homes, capacity) + key_value_pages.shape[1:], key_value_pages.dtype)
        .at[targets, place]
        .set(written[departing_slots])
    )
    arrived = lax.all_to_all(outbound, "req", split_axis=0, concat_axis=0, tiled=True)
    migrated_pool = jnp.concatenate(
        [written[:live_slots], arrived.reshape((homes * capacity,) + key_value_pages.shape[1:])],
        axis=0,
    )
    return (attention, migrated_pool)


def solution(mesh):
    in_specs = (
        P(None, "req"),
        P("req", "grp"),
        P("req", "grp", None),
        P(None, None, "grp"),
        P(),
        P("req", None),
        P("req", "grp", None, None, None),
        P("req"),
        P("req", None),
        P("req"),
        P("req", None),
    )
    out_specs = (P("req", None), P("req", "grp", None, None, None))
    return jax.shard_map(shards, mesh=mesh, in_specs=in_specs, out_specs=out_specs, check_vma=False)
```

profile of v0, /device:TPU:1, one launch (start us, length us, event | category | flops | bytes accessed | tf_op | source)
XLA Modules:
  0.0 158.4 jit_solution(13711185269570245694)
XLA Ops:
  0.7 1.5 copy.92
  2.4 0.4 convolution_bitcast_fusion
  2.8 1.1 slice.84
  3.9 0.2 copy-done.2
  4.1 0.8 fusion.11
  4.9 1.0 copy.63
  5.8 1.3 multiply_reduce_fusion
  7.2 0.7 pad_maximum_fusion.1
  7.9 1.8 %copy.43 = f32[256,256]{1,0:T(8,128)} copy(f32[256,256]{0,1:T(8,128)} %pad_maximum_fusion.1) | data formatting | bytes 524288 | tf_op jit(solution)/shard_map/concatenate | solution.py:54
  9.7 11.0 %all-to-all-start = ((f32[32,8,256]{2,1,0:T(8,128)}), f32[32,8,256]{2,1,0:T(8,128)}, u32[]{:S(2)}, u32[]{:S(2)}) async-start(f32[32,8,256]{2,1,0:T(8,128)} %bitcast.113), calls=%async_computation | async-start | bytes 524288 | tf_op jit(solution)/shard_map/all_to_all | solution.py:55
  20.8 1.8 %gather_fusion = bf16[256,2,8,128]{3,2,1,0:T(8,128)(2,1)} fusion(bf16[320,2,8,128]{3,2,1,0:T(8,128)(2,1)S(1)} %bitcast.107, s32[1024]{0:T(1024)S(1)} %pad_clamp_fusion.2), kind=kCustom, calls=%fused_computation | custom fusion | bytes 2098176 | tf_op jit(solution)/shard_map/gather | solution.py:72
  22.6 2.1 %fusion.41 = (bf16[8,32,1,8,128]{4,3,2,1,0:T(8,128)(2,1)}, bf16[8,32,1,8,128]{4,3,2,1,0:T(8,128)(2,1)S(1)}) fusion(bf16[8,32,2,8,128]{4,3,2,1,0:T(8,128)(2,1)} %bitcast.110), kind=kLoop, calls=%fused_computation.114 | loop fusion | bytes 2097152 | tf_op jit(solution)/shard_map/slice | solution.py:74
  24.8 0.5 fusion.42
  25.3 0.7 copy-done.3
  26.0 0.3 fusion.7
  26.2 2.1 %fusion.5 = f32[8,8,8,128]{3,2,1,0:T(8,128)} fusion(bf16[8,32,1,8,128]{4,3,2,1,0:T(8,128)(2,1)} %get-tuple-element.6, f32[8,8,8,32]{3,2,1,0:T(8,128)} %copy-done.3, f32[8,8,8]{2,1,0:T(8,128)S(1)} %get-tuple-element.16, pred[8,32]{1,0:T(8,128)(4,1)S(1)} %broadcast_compare_fusion), kind=kOutput, calls=%fused_computation.20 | convolution fusion | flops 4227072 | bytes 854272 | tf_op jit(solution)/shard_map/ihgn,inhd->ihgd/dot_general | solution.py:85
  28.4 1.4 all-to-all-done
  29.8 1.0 reduce_sum.48
  30.7 0.6 broadcast_in_dim.45
  31.4 12.5 %all-to-all-start.1 = ((bf16[16,8,128]{2,1,0:T(8,128)(2,1)}), bf16[16,8,128]{2,1,0:T(8,128)(2,1)}, u32[]{:S(2)}, u32[]{:S(2)}) async-start(bf16[16,8,128]{2,1,0:T(8,128)(2,1)} %broadcast_in_dim.45), calls=%async_computation.1 | async-start | bytes 65536 | tf_op jit(solution)/shard_map/all_to_all | solution.py:60
  43.9 0.6 fusion.35
  44.5 0.7 copy.41
  45.3 0.2 copy.46
  45.4 0.9 copy.45
  46.4 1.7 %reshape.115 = f32[8,16,512]{2,1,0:T(8,128)} reshape(f32[8,8,8,128]{3,2,1,0:T(8,128)} %fusion.5) | data formatting | bytes 524288 | tf_op jit(solution)/shard_map/reshape | solution.py:88
  48.0 1.8 %copy.44 = f32[8,16,512]{2,0,1:T(8,128)} copy(f32[8,16,512]{2,1,0:T(8,128)} %reshape.115) | data formatting | bytes 524288 | tf_op jit(solution)/shard_map/reshape | solution.py:88
  49.8 1.2 pad_clamp_fusion.1
  51.1 1.3 gather_fusion.2
  52.4 3.1 %all-to-all-done.1 = bf16[16,8,128]{2,1,0:T(8,128)(2,1)} async-done(((bf16[16,8,128]{2,1,0:T(8,128)(2,1)}), bf16[16,8,128]{2,1,0:T(8,128)(2,1)}, u32[]{:S(2)}, u32[]{:S(2)}) %all-to-all-start.1) | async-done | bytes 32800 | tf_op jit(solution)/shard_map/all_to_all | solution.py:60
  55.5 1.9 %gather_fusion.1 = bf16[8,128]{1,0:T(8,128)(2,1)} fusion(bf16[16,8,128]{2,1,0:T(8,128)(2,1)} %all-to-all-done.1, s32[8]{0:T(128)S(1)} %get-tuple-element.12), kind=kCustom, calls=%fused_computation.1 | custom fusion | bytes 4160 | tf_op jit(solution)/shard_map/gather | solution.py:64
  57.4 0.8 select_bitcast_fusion
  58.2 1.0 fusion.20
  59.3 1.8 %maximum_bitcast_fusion = f32[16,8,648]{2,1,0:T(8,128)} fusion(f32[8,16,128]{2,0,1:T(8,128)S(1)} %broadcast_in_dim.46, f32[8,16,4]{2,0,1:T(8,128)S(1)} %copy.46, f32[8,16,4]{2,0,1:T(8,128)S(1)} %copy.45, f32[8,16,512]{2,0,1:T(8,128)} %copy.44), kind=kLoop, calls=%fused_computation.22 | loop fusion | flops 248832 | bytes 663552 | tf_op jit(solution)/shard_map/transpose | solution.py:96
  61.1 8.4 %all-to-all-start.2 = ((f32[16,8,648]{2,1,0:T(8,128)}), f32[16,8,648]{2,1,0:T(8,128)}, u32[]{:S(2)}, u32[]{:S(2)}) async-start(f32[16,8,648]{2,1,0:T(8,128)} %maximum_bitcast_fusion), calls=%async_computation.2 | async-start | bytes 786432 | tf_op jit(solution)/shard_map/all_to_all | solution.py:97
  69.5 0.7 fusion.34
  70.2 0.6 gather_fusion.3
  70.8 0.6 shift-left_bitcast_fusion
  71.4 0.6 gather_fusion.4
  72.0 0.7 compare_select_fusion.1
  72.7 0.6 pad_clamp_fusion
  73.3 0.7 dynamic-slice_bitcast_fusion
  74.0 0.9 convert_reduce_fusion
  74.9 1.2 fusion.26
  76.1 0.7 fusion.36
  76.7 10.9 %all-to-all-done.2 = f32[16,8,648]{2,1,0:T(8,128)} async-done(((f32[16,8,648]{2,1,0:T(8,128)}), f32[16,8,648]{2,1,0:T(8,128)}, u32[]{:S(2)}, u32[]{:S(2)}) %all-to-all-start.2) | async-done | bytes 331808 | tf_op jit(solution)/shard_map/all_to_all | solution.py:97
  87.7 1.0 fusion.14
  88.7 0.6 slice_bitcast_fusion.3
  89.4 0.9 slice_reduce_fusion
  90.3 1.0 fusion.13
  91.3 0.2 copy.47
  91.6 0.7 bitcast_convert_fusion
  92.3 1.1 fusion.6
  93.5 28.5 %all_gather.3 = bf16[8,8192]{1,0:T(8,128)(2,1)} all-gather(bf16[8,512]{1,0:T(8,128)(2,1)S(1)} %fusion.15), channel_id=1, replica_groups=mesh['req'=32,'grp'=16] {'grp'}, dimensions={1}, use_global_device_ids=true | all-gather | bytes 139264 | tf_op jit(solution)/shard_map/all_gather | solution.py:126
  122.0 0.7 copy_bitcast_fusion.5
  122.7 0.7 maximum_select_fusion
  123.4 0.8 scatter_fusion
  124.3 0.7 gather_fusion.5
  125.0 0.7 broadcast.228
  125.7 3.8 %scatter_fusion.1 = bf16[32,2,2,8,128]{4,3,2,1,0:T(8,128)(2,1)} fusion(bf16[32,2,2,8,128]{4,3,2,1,0:T(8,128)(2,1)} %broadcast.228, s32[32]{0:T(128)S(1)} %fusion.36, bf16[32,2,8,128]{3,2,1,0:T(8,128)(2,1)S(1)} %gather_fusion.5), kind=kCustom, calls=%fused_computation.7 | custom fusion | bytes 393472 | tf_op jit(solution)/shard_map/scatter | solution.py:146
  129.5 16.8 %all-to-all-start.3 = ((bf16[32,2,1,2,8,128]{5,4,3,1,2,0:T(8,128)(2,1)}), bf16[32,2,1,2,8,128]{5,4,3,1,2,0:T(8,128)(2,1)}, u32[]{:S(2)}, u32[]{:S(2)}) async-start(bf16[32,2,1,2,8,128]{5,4,3,1,2,0:T(8,128)(2,1)} %bitcast.112), calls=%async_computation.3 | async-start | bytes 524288 | tf_op jit(solution)/shard_map/all_to_all | solution.py:148
  146.3 1.2 slice_bitcast_fusion
  147.4 7.8 %all-to-all-done.3 = bf16[32,2,1,2,8,128]{5,4,3,1,2,0:T(8,128)(2,1)} async-done(((bf16[32,2,1,2,8,128]{5,4,3,1,2,0:T(8,128)(2,1)}), bf16[32,2,1,2,8,128]{5,4,3,1,2,0:T(8,128)(2,1)}, u32[]{:S(2)}, u32[]{:S(2)}) %all-to-all-start.3) | async-done | bytes 262176 | tf_op jit(solution)/shard_map/all_to_all | solution.py:148
  155.2 2.5 %pad_maximum_fusion = bf16[320,1,2,8,128]{4,3,2,1,0:T(8,128)(2,1)} fusion(bf16[64,1,2,8,128]{4,3,2,1,0:T(8,128)(2,1)} %bitcast.43, bf16[256,1,2,8,128]{4,3,2,1,0:T(8,128)(2,1)} %slice_bitcast_fusion), kind=kLoop, calls=%fused_computation.9 | loop fusion | flops 655360 | bytes 2621440 | tf_op jit(solution)/shard_map/concatenate | solution.py:149
  157.7 0.7 copy.93
  (42 shorter events, 0.9 us)
Async XLA Ops:
  0.6 50.4 %copy-start = (bf16[128,64,128]{2,1,0:T(8,128)(2,1)S(1)}, bf16[128,64,128]{2,1,0:T(8,128)(2,1)}, u32[]{:S(2)}) copy-start(bf16[128,64,128]{2,1,0:T(8,128)(2,1)} %param.14) | copy-start | bytes 6291460
  0.6 1.7 %copy-start.6 = (bf16[256,256]{1,0:T(8,128)(2,1)S(1)}, bf16[256,256]{1,0:T(8,128)(2,1)}, u32[]{:S(2)}) copy-start(bf16[256,256]{1,0:T(8,128)(2,1)} %param.11) | copy-start | bytes 393220
  0.7 1.7 %copy-start.7 = (bf16[256,128]{1,0:T(8,128)(2,1)S(1)}, bf16[256,128]{1,0:T(8,128)(2,1)}, u32[]{:S(2)}) copy-start(bf16[256,128]{1,0:T(8,128)(2,1)} %param.12) | copy-start | bytes 196612
  0.7 1.6 %copy-start.4 = (bf16[256,8,128]{2,1,0:T(8,128)(2,1)S(1)}, bf16[256,8,128]{2,1,0:T(8,128)(2,1)}, u32[]{:S(2)}) copy-start(bf16[256,8,128]{2,1,0:T(8,128)(2,1)} %param.13) | copy-start | bytes 1572868
  2.7 1.4 copy-start.2
  2.8 1.4 copy-start.8
  4.1 3.1 %slice-start = ((f32[256,1152]{0,1:T(8,128)}), f32[256,128]{0,1:T(8,128)S(1)}, s32[]{:S(2)}) async-start(f32[256,1152]{0,1:T(8,128)} %copy-done.2), calls=%async_computation.4 | async-start | bytes 262144 | tf_op jit(solution)/shard_map/slice | solution.py:47
  5.8 14.9 %copy-start.1 = (s32[8,32]{1,0:T(8,128)S(1)}, s32[8,32]{1,0:T(8,128)}, u32[]{:S(2)}) copy-start(s32[8,32]{1,0:T(8,128)} %param.19) | copy-start | bytes 3076
  9.7 20.1 %all-to-all-start = ((f32[32,8,256]{2,1,0:T(8,128)}), f32[32,8,256]{2,1,0:T(8,128)}, u32[]{:S(2)}, u32[]{:S(2)}) async-start(f32[32,8,256]{2,1,0:T(8,128)} %bitcast.113), calls=%async_computation | async-start | bytes 524288 | tf_op jit(solution)/shard_map/all_to_all | solution.py:55
  22.6 2.1 %copy-start.11 = (s32[8]{0:T(128)S(1)}, s32[8]{0:T(128)}, u32[]{:S(2)}) copy-start(s32[8]{0:T(128)} %param.18) | copy-start | bytes 100
  22.6 2.2 %copy-start.10 = (bf16[8,8192]{1,0:T(8,128)(2,1)S(1)}, bf16[8,8192]{1,0:T(8,128)(2,1)}, u32[]{:S(2)}) copy-start(bf16[8,8192]{1,0:T(8,128)(2,1)} %param.16) | copy-start | bytes 393220
  24.8 19.1 %copy-start.9 = (s32[256,1]{0,1:T(1,128)S(1)}, s32[256,1]{0,1:T(1,128)}, u32[]{:S(2)}) copy-start(s32[256,1]{0,1:T(1,128)} %param.15) | copy-start | bytes 3076
  25.3 0.7 copy-start.3
  31.4 24.1 %all-to-all-start.1 = ((bf16[16,8,128]{2,1,0:T(8,128)(2,1)}), bf16[16,8,128]{2,1,0:T(8,128)(2,1)}, u32[]{:S(2)}, u32[]{:S(2)}) async-start(bf16[16,8,128]{2,1,0:T(8,128)(2,1)} %broadcast_in_dim.45), calls=%async_computation.1 | async-start | bytes 65536 | tf_op jit(solution)/shard_map/all_to_all | solution.py:60
  61.1 26.6 %all-to-all-start.2 = ((f32[16,8,648]{2,1,0:T(8,128)}), f32[16,8,648]{2,1,0:T(8,128)}, u32[]{:S(2)}, u32[]{:S(2)}) async-start(f32[16,8,648]{2,1,0:T(8,128)} %maximum_bitcast_fusion), calls=%async_computation.2 | async-start | bytes 786432 | tf_op jit(solution)/shard_map/all_to_all | solution.py:97
  129.5 25.7 %all-to-all-start.3 = ((bf16[32,2,1,2,8,128]{5,4,3,1,2,0:T(8,128)(2,1)}), bf16[32,2,1,2,8,128]{5,4,3,1,2,0:T(8,128)(2,1)}, u32[]{:S(2)}, u32[]{:S(2)}) async-start(bf16[32,2,1,2,8,128]{5,4,3,1,2,0:T(8,128)(2,1)} %bitcast.112), calls=%async_computation.3 | async-start | bytes 524288 | tf_op jit(solution)/shard_map/all_to_all | solution.py:148
  155.2 2.5 %copy-start.5 = (bf16[8,8192]{1,0:T(8,128)(2,1)S(1)}, bf16[8,8192]{1,0:T(8,128)(2,1)}, u32[]{:S(2)}) copy-start(bf16[8,8192]{1,0:T(8,128)(2,1)} %all_gather.3) | copy-start | bytes 393220
where the time goes:
time: 160 us; the launch traced here: 158 us
  starting transfers between devices  48.7 us (30%)
  local copies, waits for them, and re-layouts  32.1 us (20%)
  blocking collectives  28.5 us (18%)
  waiting for transfers between devices  23.2 us (14%)
  other arithmetic  20.9 us (13%)
  matrix products  4.13 us (3%)
    all_gather x1, blocking collectives, shards(): attention = lax.all_gather(own_attention, 'grp', axis=1, tiled=True)  28.5 us
    all_to_all x1, starting transfers between devices, shards(): lax.all_to_all(outbound, 'req', split_axis=0, concat_axis=0, tiled=True)  16.8 us
    all_to_all x1, starting transfers between devices, shards(): lax.all_to_all(jnp.broadcast_to(mid_owned[None], (groups,) + mid_owned.sh...  12.5 us
    all_to_all x1, starting transfers between devices, shards(): summed = jnp.sum(lax.all_to_all(partial, 'req', 0, 0, tiled=False), axis=0)  11 us
    all_to_all x1, waiting for transfers between devices, shards(): received = lax.all_to_all(parcel, 'grp', 0, 0, tiled=False)  10.9 us
    all_to_all x1, starting transfers between devices, shards(): received = lax.all_to_all(parcel, 'grp', 0, 0, tiled=False)  8.38 us
    all_to_all x1, waiting for transfers between devices, shards(): lax.all_to_all(outbound, 'req', split_axis=0, concat_axis=0, tiled=True)  7.77 us
    unnamed x29, local copies, waits for them, and re-layouts  4.87 us
  transfers between devices with their start and end apart: 4, of which 4 were waited for; matrix products, arithmetic and copies ran while one was open for 15% of the time, Pallas kernels for 0%

commit v1 on v0

--- a/solution.py
+++ b/solution.py
@@ -123,7 +123,9 @@
         + new_weight[..., None] * own_value.astype(jnp.float32)[:, None, :]
     )
     own_attention = (mixed / total[..., None]).astype(jnp.bfloat16).reshape(rows, mixed_width)
-    attention = lax.all_gather(own_attention, "grp", axis=1, tiled=True)
+    attention = jnp.concatenate(
+        lax.all_to_all(jnp.stack([own_attention] * lax.axis_size("grp")), "grp", 0, 0), axis=1
+    )
     page_slot = page_slot_table[request_index, lengths // page_size]
     offset = lengths % page_size
     mine = offset // slot_tokens == group_index

time: 160 us -> 143 us (0.89)
  blocking collectives: 28.5 us -> 0 us
  waiting for transfers between devices: 23.2 us -> 32 us
    all_gather x1 -> x0, blocking collectives: 28.5 us -> none  [shards(): attention = lax.all_gather(own_attention, 'grp', axis=1, tiled=True)]
    all_to_all x0 -> x1, waiting for transfers between devices: none -> 9.8 us  [shards(): lax.all_to_all(jnp.stack([own_attention] * lax.axis_size('grp')), 'grp',...]
    all_to_all x0 -> x1, starting transfers between devices: none -> 6.05 us  [shards(): lax.all_to_all(jnp.stack([own_attention] * lax.axis_size('grp')), 'grp',...]
    all_to_all x1, starting transfers between devices: 16.8 us -> 12.1 us  [shards(): lax.all_to_all(outbound, 'req', split_axis=0, concat_axis=0, tiled=True)]
    unnamed x29 -> x31, local copies, waits for them, and re-layouts: 4.87 us -> 4.86 us
  transfers between devices with their start and end apart: 4 -> 5, of which waited for: 4 -> 5; matrix products, arithmetic and copies ran while one was open for 15% -> 19% of each run, Pallas kernels for 0% -> 0%
where the time goes in v1:
time: 143 us; the launch traced here: 140 us
  starting transfers between devices  50.1 us (35%)
  waiting for transfers between devices  32 us (22%)
  local copies, waits for them, and re-layouts  31.7 us (22%)
  other arithmetic  21.3 us (15%)
  matrix products  4.13 us (3%)
    all_to_all x1, starting transfers between devices, shards(): lax.all_to_all(jnp.broadcast_to(mid_owned[None], (groups,) + mid_owned.sh...  12.5 us
    all_to_all x1, starting transfers between devices, shards(): lax.all_to_all(outbound, 'req', split_axis=0, concat_axis=0, tiled=True)  12.1 us
    all_to_all x1, starting transfers between devices, shards(): summed = jnp.sum(lax.all_to_all(partial, 'req', 0, 0, tiled=False), axis=0)  11 us
    all_to_all x1, waiting for transfers between devices, shards(): received = lax.all_to_all(parcel, 'grp', 0, 0, tiled=False)  10.9 us
    all_to_all x1, waiting for transfers between devices, shards(): lax.all_to_all(jnp.stack([own_attention] * lax.axis_size('grp')), 'grp',...  9.8 us
    all_to_all x1, starting transfers between devices, shards(): received = lax.all_to_all(parcel, 'grp', 0, 0, tiled=False)  8.49 us
    all_to_all x1, waiting for transfers between devices, shards(): lax.all_to_all(outbound, 'req', split_axis=0, concat_axis=0, tiled=True)  6.91 us
    all_to_all x1, starting transfers between devices, shards(): lax.all_to_all(jnp.stack([own_attention] * lax.axis_size('grp')), 'grp',...  6.05 us
  transfers between devices with their start and end apart: 5, of which 5 were waited for; matrix products, arithmetic and copies ran while one was open for 19% of the time, Pallas kernels for 0%

profile of v1, /device:TPU:1, one launch (start us, length us, event | category | flops | bytes accessed | tf_op | source)
XLA Modules:
  0.0 140.1 jit_solution(6995970577039890552)
XLA Ops:
  0.7 1.5 %copy.92 = bf16[320,1,2,8,128]{4,3,2,1,0:T(8,128)(2,1)S(1)} copy(bf16[320,1,2,8,128]{4,3,2,1,0:T(8,128)(2,1)} %param.17) | data formatting | bytes 2621440
  2.4 0.4 convolution_bitcast_fusion
  2.8 1.1 slice.84
  3.9 0.2 copy-done.2
  4.1 0.8 fusion.11
  4.9 1.0 copy.63
  5.8 1.3 multiply_reduce_fusion
  7.2 0.7 pad_maximum_fusion.1
  7.9 1.8 %copy.43 = f32[256,256]{1,0:T(8,128)} copy(f32[256,256]{0,1:T(8,128)} %pad_maximum_fusion.1) | data formatting | bytes 524288 | tf_op jit(solution)/shard_map/concatenate | solution.py:54
  9.7 11.0 %all-to-all-start = ((f32[32,8,256]{2,1,0:T(8,128)}), f32[32,8,256]{2,1,0:T(8,128)}, u32[]{:S(2)}, u32[]{:S(2)}) async-start(f32[32,8,256]{2,1,0:T(8,128)} %bitcast.116), calls=%async_computation | async-start | bytes 524288 | tf_op jit(solution)/shard_map/all_to_all | solution.py:55
  20.8 1.8 %gather_fusion = bf16[256,2,8,128]{3,2,1,0:T(8,128)(2,1)} fusion(bf16[320,2,8,128]{3,2,1,0:T(8,128)(2,1)S(1)} %bitcast.110, s32[1024]{0:T(1024)S(1)} %pad_clamp_fusion.2), kind=kCustom, calls=%fused_computation | custom fusion | bytes 2098176 | tf_op jit(solution)/shard_map/gather | solution.py:72
  22.6 2.1 %fusion.41 = (bf16[8,32,1,8,128]{4,3,2,1,0:T(8,128)(2,1)}, bf16[8,32,1,8,128]{4,3,2,1,0:T(8,128)(2,1)S(1)}) fusion(bf16[8,32,2,8,128]{4,3,2,1,0:T(8,128)(2,1)} %bitcast.113), kind=kLoop, calls=%fused_computation.114 | loop fusion | bytes 2097152 | tf_op jit(solution)/shard_map/slice | solution.py:74
  24.8 0.5 fusion.42
  25.2 0.7 copy-done.3
  25.9 0.3 fusion.7
  26.2 2.1 %fusion.5 = f32[8,8,8,128]{3,2,1,0:T(8,128)} fusion(bf16[8,32,1,8,128]{4,3,2,1,0:T(8,128)(2,1)} %get-tuple-element.6, f32[8,8,8,32]{3,2,1,0:T(8,128)} %copy-done.3, f32[8,8,8]{2,1,0:T(8,128)S(1)} %get-tuple-element.16, pred[8,32]{1,0:T(8,128)(4,1)S(1)} %broadcast_compare_fusion), kind=kOutput, calls=%fused_computation.20 | convolution fusion | flops 4227072 | bytes 854272 | tf_op jit(solution)/shard_map/ihgn,inhd->ihgd/dot_general | solution.py:85
  28.4 1.4 all-to-all-done
  29.7 1.0 reduce_sum.48
  30.7 0.6 broadcast_in_dim.45
  31.3 12.5 %all-to-all-start.1 = ((bf16[16,8,128]{2,1,0:T(8,128)(2,1)}), bf16[16,8,128]{2,1,0:T(8,128)(2,1)}, u32[]{:S(2)}, u32[]{:S(2)}) async-start(bf16[16,8,128]{2,1,0:T(8,128)(2,1)} %broadcast_in_dim.45), calls=%async_computation.1 | async-start | bytes 65536 | tf_op jit(solution)/shard_map/all_to_all | solution.py:60
  43.8 0.7 fusion.35
  44.5 0.7 copy.41
  45.5 0.9 copy.45
  46.4 1.7 %reshape.125 = f32[8,16,512]{2,1,0:T(8,128)} reshape(f32[8,8,8,128]{3,2,1,0:T(8,128)} %fusion.5) | data formatting | bytes 524288 | tf_op jit(solution)/shard_map/reshape | solution.py:88
  48.1 1.8 %copy.44 = f32[8,16,512]{2,0,1:T(8,128)} copy(f32[8,16,512]{2,1,0:T(8,128)} %reshape.125) | data formatting | bytes 524288 | tf_op jit(solution)/shard_map/reshape | solution.py:88
  49.9 1.3 pad_clamp_fusion.1
  51.2 1.3 gather_fusion.2
  52.5 3.0 %all-to-all-done.1 = bf16[16,8,128]{2,1,0:T(8,128)(2,1)} async-done(((bf16[16,8,128]{2,1,0:T(8,128)(2,1)}), bf16[16,8,128]{2,1,0:T(8,128)(2,1)}, u32[]{:S(2)}, u32[]{:S(2)}) %all-to-all-start.1) | async-done | bytes 32800 | tf_op jit(solution)/shard_map/all_to_all | solution.py:60
  55.5 1.9 %gather_fusion.1 = bf16[8,128]{1,0:T(8,128)(2,1)} fusion(bf16[16,8,128]{2,1,0:T(8,128)(2,1)} %all-to-all-done.1, s32[8]{0:T(128)S(1)} %get-tuple-element.12), kind=kCustom, calls=%fused_computation.1 | custom fusion | bytes 4160 | tf_op jit(solution)/shard_map/gather | solution.py:64
  57.4 0.8 select_bitcast_fusion
  58.2 1.0 fusion.20
  59.3 1.8 %maximum_bitcast_fusion = f32[16,8,648]{2,1,0:T(8,128)} fusion(f32[8,16,128]{2,0,1:T(8,128)S(1)} %broadcast_in_dim.46, f32[8,16,4]{2,0,1:T(8,128)S(1)} %copy.46, f32[8,16,4]{2,0,1:T(8,128)S(1)} %copy.45, f32[8,16,512]{2,0,1:T(8,128)} %copy.44), kind=kLoop, calls=%fused_computation.22 | loop fusion | flops 248832 | bytes 663552 | tf_op jit(solution)/shard_map/transpose | solution.py:96
  61.1 8.5 %all-to-all-start.2 = ((f32[16,8,648]{2,1,0:T(8,128)}), f32[16,8,648]{2,1,0:T(8,128)}, u32[]{:S(2)}, u32[]{:S(2)}) async-start(f32[16,8,648]{2,1,0:T(8,128)} %maximum_bitcast_fusion), calls=%async_computation.2 | async-start | bytes 786432 | tf_op jit(solution)/shard_map/all_to_all | solution.py:97
  69.6 0.7 fusion.34
  70.3 0.6 gather_fusion.3
  70.9 0.6 shift-left_bitcast_fusion
  71.5 0.6 gather_fusion.4
  72.1 0.7 compare_select_fusion.1
  72.7 0.6 pad_clamp_fusion
  73.3 0.7 dynamic-slice_bitcast_fusion
  74.0 0.9 convert_reduce_fusion
  74.9 1.3 fusion.26
  76.2 0.7 fusion.36
  76.9 10.9 %all-to-all-done.2 = f32[16,8,648]{2,1,0:T(8,128)} async-done(((f32[16,8,648]{2,1,0:T(8,128)}), f32[16,8,648]{2,1,0:T(8,128)}, u32[]{:S(2)}, u32[]{:S(2)}) %all-to-all-start.2) | async-done | bytes 331808 | tf_op jit(solution)/shard_map/all_to_all | solution.py:97
  87.8 1.0 fusion.14
  88.8 0.6 slice_bitcast_fusion.3
  89.5 0.9 slice_reduce_fusion
  90.4 1.0 fusion.13
  91.4 0.8 copy.47
  92.2 0.6 fusion.40
  92.8 0.8 maximum_select_fusion
  93.5 0.8 scatter_fusion
  94.4 0.7 gather_fusion.5
  95.1 0.7 broadcast.232
  95.8 3.8 %scatter_fusion.1 = bf16[32,2,2,8,128]{4,3,2,1,0:T(8,128)(2,1)} fusion(bf16[32,2,2,8,128]{4,3,2,1,0:T(8,128)(2,1)} %broadcast.232, s32[32]{0:T(128)S(1)} %fusion.36, bf16[32,2,8,128]{3,2,1,0:T(8,128)(2,1)S(1)} %gather_fusion.5), kind=kCustom, calls=%fused_computation.7 | custom fusion | bytes 393472 | tf_op jit(solution)/shard_map/scatter | solution.py:148
  99.6 12.1 %all-to-all-start.4 = ((bf16[32,2,1,2,8,128]{5,4,3,1,2,0:T(8,128)(2,1)}), bf16[32,2,1,2,8,128]{5,4,3,1,2,0:T(8,128)(2,1)}, u32[]{:S(2)}, u32[]{:S(2)}) async-start(bf16[32,2,1,2,8,128]{5,4,3,1,2,0:T(8,128)(2,1)} %bitcast.115), calls=%async_computation.4 | async-start | bytes 524288 | tf_op jit(solution)/shard_map/all_to_all | solution.py:150
  111.7 1.1 fusion.6
  112.8 0.7 bitcast_convert_fusion
  113.7 6.9 %all-to-all-done.4 = bf16[32,2,1,2,8,128]{5,4,3,1,2,0:T(8,128)(2,1)} async-done(((bf16[32,2,1,2,8,128]{5,4,3,1,2,0:T(8,128)(2,1)}), bf16[32,2,1,2,8,128]{5,4,3,1,2,0:T(8,128)(2,1)}, u32[]{:S(2)}, u32[]{:S(2)}) %all-to-all-start.4) | async-done | bytes 262176 | tf_op jit(solution)/shard_map/all_to_all | solution.py:150
  120.6 0.7 stack.6
  121.3 6.0 %all-to-all-start.3 = ((bf16[16,8,512]{2,1,0:T(8,128)(2,1)}), bf16[16,8,512]{2,1,0:T(8,128)(2,1)S(1)}, u32[]{:S(2)}, u32[]{:S(2)}) async-start(bf16[16,8,512]{2,1,0:T(8,128)(2,1)} %stack.6), calls=%async_computation.3 | async-start | bytes 262144 | tf_op jit(solution)/shard_map/all_to_all | solution.py:127
  127.5 2.1 %pad_maximum_fusion = bf16[320,1,2,8,128]{4,3,2,1,0:T(8,128)(2,1)} fusion(bf16[64,1,2,8,128]{4,3,2,1,0:T(8,128)(2,1)} %bitcast.45, bf16[256,1,2,8,128]{4,3,2,1,0:T(8,128)(2,1)S(1)} %slice_bitcast_fusion), kind=kLoop, calls=%fused_computation.9 | loop fusion | flops 655360 | bytes 2621440 | tf_op jit(solution)/shard_map/concatenate | solution.py:151
  129.6 9.8 %all-to-all-done.3 = bf16[16,8,512]{2,1,0:T(8,128)(2,1)S(1)} async-done(((bf16[16,8,512]{2,1,0:T(8,128)(2,1)}), bf16[16,8,512]{2,1,0:T(8,128)(2,1)S(1)}, u32[]{:S(2)}, u32[]{:S(2)}) %all-to-all-start.3) | async-done | bytes 131104 | tf_op jit(solution)/shard_map/all_to_all | solution.py:127
  139.4 0.7 copy.93
  (46 shorter events, 1.3 us)
Async XLA Ops:
  0.6 50.5 %copy-start = (bf16[128,64,128]{2,1,0:T(8,128)(2,1)S(1)}, bf16[128,64,128]{2,1,0:T(8,128)(2,1)}, u32[]{:S(2)}) copy-start(bf16[128,64,128]{2,1,0:T(8,128)(2,1)} %param.14) | copy-start | bytes 6291460
  0.6 1.7 %copy-start.5 = (bf16[256,256]{1,0:T(8,128)(2,1)S(1)}, bf16[256,256]{1,0:T(8,128)(2,1)}, u32[]{:S(2)}) copy-start(bf16[256,256]{1,0:T(8,128)(2,1)} %param.11) | copy-start | bytes 393220
  0.7 1.7 %copy-start.6 = (bf16[256,128]{1,0:T(8,128)(2,1)S(1)}, bf16[256,128]{1,0:T(8,128)(2,1)}, u32[]{:S(2)}) copy-start(bf16[256,128]{1,0:T(8,128)(2,1)} %param.12) | copy-start | bytes 196612
  0.7 1.6 %copy-start.4 = (bf16[256,8,128]{2,1,0:T(8,128)(2,1)S(1)}, bf16[256,8,128]{2,1,0:T(8,128)(2,1)}, u32[]{:S(2)}) copy-start(bf16[256,8,128]{2,1,0:T(8,128)(2,1)} %param.13) | copy-start | bytes 1572868
  2.7 1.4 copy-start.2
  2.8 1.4 copy-start.9
  4.1 3.1 %slice-start = ((f32[256,1152]{0,1:T(8,128)}), f32[256,128]{0,1:T(8,128)S(1)}, s32[]{:S(2)}) async-start(f32[256,1152]{0,1:T(8,128)} %copy-done.2), calls=%async_computation.5 | async-start | bytes 262144 | tf_op jit(solution)/shard_map/slice | solution.py:47
  5.8 14.9 %copy-start.1 = (s32[8,32]{1,0:T(8,128)S(1)}, s32[8,32]{1,0:T(8,128)}, u32[]{:S(2)}) copy-start(s32[8,32]{1,0:T(8,128)} %param.19) | copy-start | bytes 3076
  9.7 20.1 %all-to-all-start = ((f32[32,8,256]{2,1,0:T(8,128)}), f32[32,8,256]{2,1,0:T(8,128)}, u32[]{:S(2)}, u32[]{:S(2)}) async-start(f32[32,8,256]{2,1,0:T(8,128)} %bitcast.116), calls=%async_computation | async-start | bytes 524288 | tf_op jit(solution)/shard_map/all_to_all | solution.py:55
  22.6 2.1 %copy-start.12 = (s32[8]{0:T(128)S(1)}, s32[8]{0:T(128)}, u32[]{:S(2)}) copy-start(s32[8]{0:T(128)} %param.18) | copy-start | bytes 100
  22.6 2.2 %copy-start.11 = (bf16[8,8192]{1,0:T(8,128)(2,1)S(1)}, bf16[8,8192]{1,0:T(8,128)(2,1)}, u32[]{:S(2)}) copy-start(bf16[8,8192]{1,0:T(8,128)(2,1)} %param.16) | copy-start | bytes 393220
  24.8 19.1 %copy-start.10 = (s32[256,1]{0,1:T(1,128)S(1)}, s32[256,1]{0,1:T(1,128)}, u32[]{:S(2)}) copy-start(s32[256,1]{0,1:T(1,128)} %param.15) | copy-start | bytes 3076
  25.2 0.7 copy-start.3
  31.3 24.1 %all-to-all-start.1 = ((bf16[16,8,128]{2,1,0:T(8,128)(2,1)}), bf16[16,8,128]{2,1,0:T(8,128)(2,1)}, u32[]{:S(2)}, u32[]{:S(2)}) async-start(bf16[16,8,128]{2,1,0:T(8,128)(2,1)} %broadcast_in_dim.45), calls=%async_computation.1 | async-start | bytes 65536 | tf_op jit(solution)/shard_map/all_to_all | solution.py:60
  61.1 26.7 %all-to-all-start.2 = ((f32[16,8,648]{2,1,0:T(8,128)}), f32[16,8,648]{2,1,0:T(8,128)}, u32[]{:S(2)}, u32[]{:S(2)}) async-start(f32[16,8,648]{2,1,0:T(8,128)} %maximum_bitcast_fusion), calls=%async_computation.2 | async-start | bytes 786432 | tf_op jit(solution)/shard_map/all_to_all | solution.py:97
  92.8 20.7 %copy-start.8 = (f32[8,4]{1,0:T(8,128)S(1)}, f32[8,4]{1,0:T(8,128)}, u32[]{:S(2)}) copy-start(f32[8,4]{1,0:T(8,128)} %get-tuple-element.2) | copy-start | bytes 388
  92.8 20.8 %copy-start.7 = (f32[8,4]{1,0:T(8,128)S(1)}, f32[8,4]{1,0:T(8,128)}, u32[]{:S(2)}) copy-start(f32[8,4]{1,0:T(8,128)} %get-tuple-element.3) | copy-start | bytes 388
  99.6 21.0 %all-to-all-start.4 = ((bf16[32,2,1,2,8,128]{5,4,3,1,2,0:T(8,128)(2,1)}), bf16[32,2,1,2,8,128]{5,4,3,1,2,0:T(8,128)(2,1)}, u32[]{:S(2)}, u32[]{:S(2)}) async-start(bf16[32,2,1,2,8,128]{5,4,3,1,2,0:T(8,128)(2,1)} %bitcast.115), calls=%async_computation.4 | async-start | bytes 524288 | tf_op jit(solution)/shard_map/all_to_all | solution.py:150
  121.3 18.2 %all-to-all-start.3 = ((bf16[16,8,512]{2,1,0:T(8,128)(2,1)}), bf16[16,8,512]{2,1,0:T(8,128)(2,1)S(1)}, u32[]{:S(2)}, u32[]{:S(2)}) async-start(bf16[16,8,512]{2,1,0:T(8,128)(2,1)} %stack.6), calls=%async_computation.3 | async-start | bytes 262144 | tf_op jit(solution)/shard_map/all_to_all | solution.py:127
